TPU v7x, 128 devices: a whole 4x4x4 slice. The times are simulated.
128 devices in a mesh: row: 4 (over x), col: 32 (over z, y, core).
Axes of the slice: x: 4, y: 4, z: 4, core: 2. Of those that a mesh axis runs over, the one named last changes fastest.
Arguments:
- child_factors: bfloat16 [2, 2048, 8192], P(None, 'col', 'row'), may hold values from -0.0625 to 0.0625
- child_tiles: int32 [2, 16], replicated, may hold values from 0 to 63, as said below
- root_diag: float32 [8192], P('col'), may hold values from 0.5 to 4
Outputs:
- front_out: float32 [8192, 8192], P('row', 'col')
Inputs may be any that keep to these rules, and one draw needn't show every extreme that they name: `child_tiles`: each row lists 2048 / 128 distinct root tiles in increasing order; the first child's list holds tile 0 and the second child's holds the last tile. For every r below 4, exactly 2048 / (128 * 4) tiles t of each row have ((t * 128) // 256) % 4 == r.
All inputs are finite; a program needn't handle non-finite values.
Results may differ from a plain program's by a relative error of at most 0.0003.
Values may be sent and summed in bfloat16 or wider, within the bound.
No kernel may reach another device: no remote copies, remote signals or barrier semaphores. Data moves between devices by JAX's collectives and lax.ppermute only.
A program may use at most 128 MiB of HBM per device.

v0:
```python
import jax
import jax.numpy as jnp
from jax import lax
from jax.sharding import PartitionSpec as P

TILE = 128
NPAN = 1


def broadcast(block, axis, source):
    block = jnp.where(lax.axis_index(axis) == source, block, jnp.zeros_like(block))
    return lax.psum(block, axis)


def pivot_factor(source, local_block, owner_row, block_size, identity, usable):
    diag_rows = source[local_block * block_size : (local_block + 1) * block_size]
    pivots = broadcast(diag_rows, "row", owner_row)
    return jnp.linalg.cholesky(jnp.where(usable, pivots, identity))


def solve_panel(source, factor, row_block, panel_step, blocks_here):
    solved = lax.linalg.triangular_solve(
        factor, source, left_side=False, lower=True, transpose_a=True
    )
    repeated = jnp.tile(jnp.tril(factor), (blocks_here, 1))
    later = (row_block > panel_step)[:, None]
    current = (row_block == panel_step)[:, None]
    return jnp.where(later, solved, jnp.where(current, repeated, 0.0))


def shards(child_factors, child_tiles, root_diag):
    highest = lax.Precision.HIGHEST
    row_count = lax.axis_size("row")
    col_count = lax.axis_size("col")
    block_size = root_diag.shape[0]
    order_total = block_size * col_count
    loc_rows = order_total // row_count
    blocks_here = loc_rows // block_size
    row_index = lax.axis_index("row")
    col_index = lax.axis_index("col")
    gathered = lax.all_gather(child_factors, "col", axis=1, tiled=True)
    tile_total = gathered.shape[1] // TILE
    tiles_per_col = block_size // TILE
    wanted = col_index * tiles_per_col + jnp.arange(tiles_per_col, dtype=jnp.int32)
    selector = (child_tiles[:, :, None] == wanted[None, None, :]).astype(jnp.bfloat16)
    tiled_rows = gathered.reshape(2, tile_total, TILE, gathered.shape[2])
    own_cols = jnp.einsum(
        "cui,cutk->citk", selector, tiled_rows, preferred_element_type=jnp.float32
    )
    own_cols = own_cols.astype(jnp.bfloat16).reshape(2, block_size, gathered.shape[2])
    partial_gram = jnp.einsum(
        "cnk,cmk->cnm", gathered, own_cols, preferred_element_type=jnp.float32
    )
    gram_tiles = partial_gram.reshape(2, tile_total, TILE, block_size)
    stored_tile = jnp.arange(lax.axis_size("row") * loc_rows // TILE, dtype=jnp.int32)
    stored_row = stored_tile * TILE
    owning = stored_row // loc_rows
    within = stored_row % loc_rows
    global_row = (owning + within // block_size * row_count) * block_size + within % block_size
    global_tile = global_row // TILE
    matches = (child_tiles[:, :, None] == global_tile[None, None, :]).astype(jnp.float32)
    placed = jnp.einsum("cus,cutm->stm", matches, gram_tiles, precision=highest)
    assembled = lax.psum_scatter(
        placed.reshape(lax.axis_size("row") * loc_rows, block_size),
        "row",
        scatter_dimension=0,
        tiled=True,
    )
    local_rows = jnp.arange(loc_rows, dtype=jnp.int32)
    row_block = row_index + local_rows // block_size * row_count
    glob_rows = row_block * block_size + local_rows % block_size
    glob_cols = col_index * block_size + jnp.arange(block_size, dtype=jnp.int32)
    front_now = assembled + jnp.where(
        glob_rows[:, None] == glob_cols[None, :], root_diag[None, :], 0.0
    )
    identity = jnp.eye(block_size, dtype=jnp.float32)
    owner_row = 0 % row_count
    local_block = 0 // row_count
    factor = pivot_factor(front_now, local_block, owner_row, block_size, identity, col_index == 0)
    own_panel = solve_panel(front_now, factor, row_block, 0, blocks_here)
    panel_block = broadcast(own_panel, "col", 0)
    own_block = lax.dynamic_slice_in_dim(
        panel_block, col_index // row_count * block_size, block_size, 0
    )
    across = broadcast(own_block.astype(jnp.bfloat16), "row", col_index % row_count).astype(
        own_block.dtype
    )
    update = jnp.dot(panel_block, across.T, precision=highest)
    front_now = jnp.where(col_index == 0, panel_block, front_now - update)
    upper_part = (row_block[:, None] < NPAN) & (col_index >= NPAN)
    return jnp.where(upper_part, 0.0, front_now)


def solution(mesh):
    placed = (P(None, "col", "row"), P(), P("col"))
    return jax.shard_map(
        shards, mesh=mesh, in_specs=placed, out_specs=P("row", "col"), check_vma=False
    )
```

profile of v0, /device:TPU:0, one launch (start us, length us, event | category | flops | bytes accessed | tf_op | source)
XLA Modules:
  0.0 501.5 jit_solution(1409809897628505502)
XLA Ops:
  6.5 0.7 all-gather.2.cloned.1.call-update
  7.3 0.0 reduce-scatter.2.cloned.1.call-start
  7.4 77.5 %all-gather.2.cloned.1.call-done = bf16[2,2048,2048]{2,1,0:T(8,128)(2,1)} async-done(((bf16[2,64,2048]{2,1,0:T(8,128)(2,1)}), bf16[2,2048,2048]{2,1,0:T(8,128)(2,1)}) %all-gather.2.cloned.1.call-update) | async-done | bytes 16777232 | tf_op jit(solution)/shard_map/all_gather | solution.py:41
  84.8 24.6 %fusion.2 = bf16[2,2,128,2048]{3,1,2,0:T(2,128)(2,1)S(1)} fusion(bf16[2,16,128,2048]{3,2,1,0:T(8,128)(2,1)} %bitcast.68, s32[2,16]{1,0:T(2,128)} %param.4, s32[2]{0:T(128)S(1)} %iota_add_fusion.1), kind=kOutput, calls=%fused_computation.5 | convolution fusion | flops 34603072 | bytes 18874504 | tf_op jit(solution)/shard_map/cui,cutk->citk/dot_general | solution.py:47
  109.5 2.2 copy.14
  111.7 13.0 %fusion.43 = f32[2,256,2048]{2,1,0:T(8,128)} fusion(bf16[2,256,2048]{2,1,0:T(8,128)(2,1)} %bitcast.73, bf16[2,2048,2048]{2,1,0:T(8,128)(2,1)} %all-gather.2.cloned.1.call-done), kind=kOutput, calls=%fused_computation.88 | convolution fusion | flops 4294967296 | bytes 23068672 | tf_op jit(solution)/shard_map/cnk,cmk->cnm/dot_general | solution.py:51
  124.7 3.1 copy.31
  127.9 3.6 fusion.21
  131.5 11.1 %copy.39 = f32[32,8,64,128]{3,1,2,0:T(8,128)} copy(f32[32,8,64,128]{3,2,1,0:T(8,128)S(1)} %bitcast.67) | data formatting | bytes 16777216
  142.6 0.0 all-reduce.5.cloned.1.call-start
  142.7 80.0 %reduce-scatter.2.cloned.1.call-done = f32[2048,256]{0,1:T(8,128)} async-done(((f32[8192,256]{0,1:T(8,128)}), f32[2048,256]{0,1:T(8,128)}) %reduce-scatter.2.cloned.1.call-update) | async-done | bytes 2097168 | tf_op jit(solution)/shard_map/reduce_scatter | solution.py:63
  222.7 1.9 select_add_fusion
  224.5 0.7 slice_select_fusion
  225.3 0.0 all-reduce.7.cloned.1.call-start
  225.4 41.6 %all-reduce.5.cloned.1.call-done = f32[256,256]{0,1:T(8,128)} async-done(((f32[256,256]{0,1:T(8,128)}), f32[256,256]{0,1:T(8,128)}) %all-reduce.5.cloned.1.call-update) | async-done | bytes 262160 | tf_op jit(solution)/shard_map/psum | solution.py:12
  267.0 1.0 convert_select_fusion
  267.9 0.1 copy.17
  268.1 1.0 fusion.10
  269.1 11.7 %cholesky.49 = f32[128,128]{1,0:T(8,128)S(1)} custom-call(f32[128,128]{1,0:T(8,128)S(1)} %cholesky.115), custom_call_target="Cholesky" | custom-call | tf_op jit(solution)/shard_map/jit(cholesky)/cholesky | solution.py:18
  280.8 9.8 %custom-call.14 = f32[1,128,128]{1,2,0:T(8,128)S(1)} custom-call(f32[1,128,128]{2,1,0:T(8,128)S(1)} %get-tuple-element.32), custom_call_target="InvertDiagBlocksLowerTriangular" | custom-call | tf_op jit(solution)/shard_map/jit(cholesky)/cholesky | solution.py:18
  290.7 0.2 fusion.14
  290.9 0.3 convolution_subtract_fusion.2
  291.1 11.7 %cholesky.103 = f32[128,128]{1,0:T(8,128)S(1)} custom-call(f32[128,128]{1,0:T(8,128)S(1)} %convolution_subtract_fusion.2), custom_call_target="Cholesky" | custom-call | tf_op jit(solution)/shard_map/jit(cholesky)/cholesky | solution.py:18
  302.9 0.1 copy.20
  303.0 0.1 copy.19
  303.1 0.1 copy.18
  303.2 0.7 compare_reduce_fusion
  305.4 0.1 tile.4
  305.5 2.2 copy.33
  307.7 0.1 triangular_solve.61
  307.8 4.5 while.1
  308.0 0.7 fusion.54
  308.7 1.3 dynamic-slice.7
  310.0 0.1 copy.41
  310.2 0.7 fusion.54
  310.8 1.3 dynamic-slice.7
  312.2 0.1 copy.41
  312.3 19.7 %custom-call.15 = f32[2,128,128]{1,2,0:T(8,128)S(1)} custom-call(f32[2,128,128]{2,1,0:T(8,128)S(1)} %get-tuple-element.12), custom_call_target="InvertDiagBlocksLowerTriangular" | custom-call | tf_op jit(solution)/shard_map/triangular_solve | solution.py:22
  332.0 1.1 fusion.8
  333.1 1.1 convolution_subtract_fusion.1
  334.2 1.1 fusion.12
  335.3 1.7 fusion.7
  337.0 0.0 all-reduce.9.cloned.1.call-start
  337.1 106.4 %all-reduce.7.cloned.1.call-done = f32[2048,256]{0,1:T(8,128)} async-done(((f32[2048,256]{0,1:T(8,128)}), f32[2048,256]{0,1:T(8,128)}) %all-reduce.7.cloned.1.call-update) | async-done | bytes 2097168 | tf_op jit(solution)/shard_map/psum | solution.py:12
  443.5 1.6 fusion.11
  445.1 41.5 %all-reduce.9.cloned.1.call-done = bf16[256,256]{0,1:T(8,128)(2,1)} async-done(((bf16[256,256]{0,1:T(8,128)(2,1)}), bf16[256,256]{0,1:T(8,128)(2,1)}) %all-reduce.9.cloned.1.call-update) | async-done | bytes 131088 | tf_op jit(solution)/shard_map/psum | solution.py:12
  486.7 5.0 fusion.6
  491.6 2.9 copy.23
  (30 shorter events, 0.3 us)
Async XLA Ops:
  6.5 78.3 %all-gather.2.cloned.1.call-start = ((), (), s32[]{:S(2)}) async-start(), calls=%async_computation.1 | async-start | bytes 17301504 | tf_op jit(solution)/shard_map/all_gather | solution.py:41
  7.3 215.4 %reduce-scatter.2.cloned.1.call-start = ((), (), s32[]{:S(2)}) async-start(), calls=%async_computation.2 | async-start | bytes 10485760 | tf_op jit(solution)/shard_map/reduce_scatter | solution.py:63
  124.7 3.1 copy-start.1
  142.6 80.1 %copy-start.2 = (f32[256]{0:T(256)S(1)}, f32[256]{0:T(256)}, u32[]{:S(2)}) copy-start(f32[256]{0:T(256)} %param.5) | copy-start | bytes 3076
  142.6 124.4 %all-reduce.5.cloned.1.call-start = ((), (), s32[]{:S(2)}) async-start(), calls=%async_computation.3 | async-start | bytes 524288 | tf_op jit(solution)/shard_map/psum | solution.py:12
  225.3 218.2 %all-reduce.7.cloned.1.call-start = ((), (), s32[]{:S(2)}) async-start(), calls=%async_computation.4 | async-start | bytes 4194304 | tf_op jit(solution)/shard_map/psum | solution.py:12
  333.1 2.2 copy-start
  337.0 149.7 %all-reduce.9.cloned.1.call-start = ((), (), s32[]{:S(2)}) async-start(), calls=%async_computation.5 | async-start | bytes 262144 | tf_op jit(solution)/shard_map/psum | solution.py:12
Sparse Core Ops, SparseCore 0:
  9.6 75.1 all-gather.1
  142.7 79.8 reduce-scatter.1
  225.4 41.5 all-reduce.4
  337.1 106.3 all-reduce.6
  445.6 40.9 all-reduce.8
where the time goes:
time: 510 us; the launch traced here: 501 us
  waiting for transfers between devices  348 us (68%)
  other arithmetic  61.7 us (12%)
  matrix products  50 us (10%)
  local copies, waits for them, and re-layouts  26.4 us (5%)
  between operations  15.2 us (3%)
    psum x3, waiting for transfers between devices, broadcast(): return lax.psum(block, axis)  190 us
    reduce_scatter x1, waiting for transfers between devices, shards(): lax.psum_scatter(placed.reshape(lax.axis_size('row') * loc_rows, block_si...  80 us
    all_gather x1, waiting for transfers between devices, shards(): gathered = lax.all_gather(child_factors, 'col', axis=1, tiled=True)  77.5 us
    another operation x6, other arithmetic, pivot_factor(): return jnp.linalg.cholesky(jnp.where(usable, pivots, identity))  34 us
    dot_general x1, matrix products, shards(): jnp.einsum('cui,cutk->citk', selector, tiled_rows, preferred_element_type...  24.6 us
    another operation x3, other arithmetic, solve_panel(): lax.linalg.triangular_solve(factor, source, left_side=False, lower=True,...  19.7 us
    unnamed x9, local copies, waits for them, and re-layouts  16.4 us
    dot_general x1, matrix products, shards(): jnp.einsum('cnk,cmk->cnm', gathered, own_cols, preferred_element_type=jnp...  13 us
  transfers between devices with their start and end apart: 5, of which 5 were waited for; matrix products, arithmetic and copies ran while one was open for 0% of the time, Pallas kernels for 0%

commit v1 on v0

--- a/solution.py
+++ b/solution.py
@@ -9,7 +9,7 @@
 
 def broadcast(block, axis, source):
     block = jnp.where(lax.axis_index(axis) == source, block, jnp.zeros_like(block))
-    return lax.psum(block, axis)
+    return jnp.sum(lax.all_gather(block, axis), axis=0)
 
 
 def pivot_factor(source, local_block, owner_row, block_size, identity, usable):

time: 510 us -> 589 us (1.15)
  waiting for transfers between devices: 348 us -> 383 us
  other arithmetic: 61.7 us -> 82.2 us
  blocking collectives: 0 us -> 13.1 us
  local copies, waits for them, and re-layouts: 26.4 us -> 33.9 us
    all_gather x0 -> x2, waiting for transfers between devices: none -> 225 us  [broadcast(): return jnp.sum(lax.all_gather(block, axis), axis=0)]
    psum x3 -> x0, waiting for transfers between devices: 190 us -> none  [broadcast(): return lax.psum(block, axis)]
    unnamed x1 -> x2, other arithmetic: 0.01 us -> 22.2 us
    all_gather x0 -> x1, blocking collectives: none -> 13.1 us  [broadcast(): return jnp.sum(lax.all_gather(block, axis), axis=0)]
    unnamed x9 -> x8, local copies, waits for them, and re-layouts: 16.4 us -> 5.14 us
    dot_general x0 -> x1, local copies, waits for them, and re-layouts: none -> 8.08 us  [shards(): placed = jnp.einsum('cus,cutm->stm', matches, gram_tiles, precision=highest)]
  transfers between devices with their start and end apart: 5 -> 4, of which waited for: 5 -> 4; matrix products, arithmetic and copies ran while one was open for 0% -> 0% of each run, Pallas kernels for 0% -> 0%
where the time goes in v1:
time: 589 us; the launch traced here: 580 us
  waiting for transfers between devices  383 us (65%)
  other arithmetic  82.2 us (14%)
  matrix products  52.2 us (9%)
  local copies, waits for them, and re-layouts  33.9 us (6%)
  between operations  14.9 us (3%)
  blocking collectives  13.1 us (2%)
    all_gather x2, waiting for transfers between devices, broadcast(): return jnp.sum(lax.all_gather(block, axis), axis=0)  225 us
    reduce_scatter x1, waiting for transfers between devices, shards(): lax.psum_scatter(placed.reshape(lax.axis_size('row') * loc_rows, block_si...  80 us
    all_gather x1, waiting for transfers between devices, shards(): gathered = lax.all_gather(child_factors, 'col', axis=1, tiled=True)  77.5 us
    another operation x6, other arithmetic, pivot_factor(): return jnp.linalg.cholesky(jnp.where(usable, pivots, identity))  34 us
    dot_general x1, matrix products, shards(): jnp.einsum('cui,cutk->citk', selector, tiled_rows, preferred_element_type...  24.5 us
    unnamed x2, other arithmetic  22.2 us
    another operation x3, other arithmetic, solve_panel(): lax.linalg.triangular_solve(factor, source, left_side=False, lower=True,...  19.7 us
    all_gather x1, blocking collectives, broadcast(): return jnp.sum(lax.all_gather(block, axis), axis=0)  13.1 us
  transfers between devices with their start and end apart: 4, of which 4 were waited for; matrix products, arithmetic and copies ran while one was open for 0% of the time, Pallas kernels for 0%

profile of v1, /device:TPU:0, one launch (start us, length us, event | category | flops | bytes accessed | tf_op | source)
XLA Modules:
  0.0 580.1 jit_solution(9197356112321010637)
XLA Ops:
  6.5 0.7 all-gather.6.cloned.1.call-update
  7.3 0.0 reduce-scatter.2.cloned.1.call-start
  7.4 77.5 %all-gather.6.cloned.1.call-done = bf16[2,2048,2048]{2,1,0:T(8,128)(2,1)} async-done(((bf16[2,64,2048]{2,1,0:T(8,128)(2,1)}), bf16[2,2048,2048]{2,1,0:T(8,128)(2,1)}) %all-gather.6.cloned.1.call-update) | async-done | bytes 16777232 | tf_op jit(solution)/shard_map/all_gather | solution.py:41
  84.8 24.5 %fusion.2 = bf16[2,2,128,2048]{3,1,2,0:T(2,128)(2,1)S(1)} fusion(bf16[2,16,128,2048]{3,2,1,0:T(8,128)(2,1)} %bitcast.68, s32[2,16]{1,0:T(2,128)} %param.4, s32[2]{0:T(128)S(1)} %iota_add_fusion.1), kind=kOutput, calls=%fused_computation.5 | convolution fusion | flops 34603072 | bytes 18874504 | tf_op jit(solution)/shard_map/cui,cutk->citk/dot_general | solution.py:47
  109.3 2.2 copy.26
  111.5 13.1 %fusion.41 = f32[2,256,2048]{2,1,0:T(8,128)} fusion(bf16[2,256,2048]{2,1,0:T(8,128)(2,1)} %bitcast.72, bf16[2,2048,2048]{2,1,0:T(8,128)(2,1)} %all-gather.6.cloned.1.call-done), kind=kOutput, calls=%fused_computation.88 | convolution fusion | flops 4294967296 | bytes 23068672 | tf_op jit(solution)/shard_map/cnk,cmk->cnm/dot_general | solution.py:51
  124.6 5.0 copy.38
  129.6 5.6 copy.27
  135.3 5.5 convolution_bitcast_fusion
  140.8 8.1 %copy.28 = f32[64,128,256]{2,1,0:T(8,128)} copy(f32[64,128,256]{2,0,1:T(8,128)S(1)} %convolution_bitcast_fusion) | data formatting | bytes 16777216 | tf_op jit(solution)/shard_map/cus,cutm->stm/dot_general | solution.py:62
  148.9 0.0 all-gather.10.cloned.1.call-start
  149.0 80.0 %reduce-scatter.2.cloned.1.call-done = f32[2048,256]{1,0:T(8,128)} async-done(((f32[8192,256]{1,0:T(8,128)}), f32[2048,256]{1,0:T(8,128)}) %reduce-scatter.2.cloned.1.call-update) | async-done | bytes 2097168 | tf_op jit(solution)/shard_map/reduce_scatter | solution.py:63
  229.0 1.8 select_add_fusion
  230.8 0.7 slice_select_fusion
  231.5 0.4 all-gather.8.cloned.1.call-start
  232.0 23.5 %all-gather.10.cloned.1.call-done = f32[1024,256]{1,0:T(8,128)} async-done(((f32[256,256]{1,0:T(8,128)}), f32[1024,256]{1,0:T(8,128)}) %all-gather.10.cloned.1.call-update) | async-done | bytes 1048592 | tf_op jit(solution)/shard_map/all_gather | solution.py:12
  255.5 1.3 reduce_sum.32
  256.8 0.1 copy.29
  256.9 0.1 fusion.11
  257.0 11.7 %cholesky.49 = f32[128,128]{1,0:T(8,128)S(1)} custom-call(f32[128,128]{1,0:T(8,128)S(1)} %cholesky.115), custom_call_target="Cholesky" | custom-call | tf_op jit(solution)/shard_map/jit(cholesky)/cholesky | solution.py:18
  268.8 9.8 %custom-call.14 = f32[1,128,128]{1,2,0:T(8,128)S(1)} custom-call(f32[1,128,128]{2,1,0:T(8,128)S(1)} %get-tuple-element.26), custom_call_target="InvertDiagBlocksLowerTriangular" | custom-call | tf_op jit(solution)/shard_map/jit(cholesky)/cholesky | solution.py:18
  278.6 0.2 constant_dynamic-update-slice_fusion.1
  278.8 0.3 convolution_subtract_fusion.2
  279.1 11.7 %cholesky.103 = f32[128,128]{1,0:T(8,128)S(1)} custom-call(f32[128,128]{1,0:T(8,128)S(1)} %convolution_subtract_fusion.2), custom_call_target="Cholesky" | custom-call | tf_op jit(solution)/shard_map/jit(cholesky)/cholesky | solution.py:18
  290.8 0.7 compare_reduce_fusion
  292.9 0.1 copy.30
  293.1 1.5 tile.4
  294.5 2.9 tile.10
  297.4 0.1 triangular_solve.68
  297.5 3.9 while.1
  297.5 0.6 fusion.52
  298.1 1.3 bitcast_dynamic-update-slice_fusion.2
  299.5 0.6 fusion.52
  300.0 1.3 bitcast_dynamic-update-slice_fusion.2
  301.4 19.7 %custom-call.15 = f32[2,128,128]{1,2,0:T(8,128)S(1)} custom-call(f32[2,128,128]{2,1,0:T(8,128)S(1)} %get-tuple-element.12), custom_call_target="InvertDiagBlocksLowerTriangular" | custom-call | tf_op jit(solution)/shard_map/triangular_solve | solution.py:22
  321.1 1.1 fusion.8
  322.2 1.8 convolution_subtract_fusion.1
  324.0 1.1 convolution_bitcast_fusion.1
  325.1 1.7 fusion.7
  326.8 2.9 copy.31
  329.8 201.6 %all-gather.8.cloned.1.call-done = f32[32,2048,256]{2,1,0:T(8,128)} async-done(((f32[1,2048,256]{2,1,0:T(8,128)}), f32[32,2048,256]{2,1,0:T(8,128)}) %all-gather.8.cloned.1.call-update) | async-done | bytes 67108880 | tf_op jit(solution)/shard_map/all_gather | solution.py:12
  531.4 22.2 %reduce_sum.34 = f32[2048,256]{1,0:T(8,128)} reduce(f32[32,2048,256]{2,1,0:T(8,128)} %all-gather.8.cloned.1.call-done, f32[]{:T(128)} %constant.197.clone.1), dimensions={0}, to_apply=%region_6.7 | reduce | flops 16252928 | bytes 69206016
  553.5 1.0 constant_dynamic-slice_fusion.1
  554.5 0.1 copy.37
  554.6 13.1 %all-gather.1 = bf16[1024,256]{0,1:T(8,128)(2,1)S(1)} all-gather(bf16[256,256]{0,1:T(8,128)(2,1)S(1)} %convert_select_fusion), channel_id=3, replica_groups=mesh['row'=4,'col'=32] {'row'}, dimensions={0}, use_global_device_ids=true | all-gather | bytes 655360 | tf_op jit(solution)/shard_map/all_gather | solution.py:12
  567.7 0.4 reshape.261
  568.1 0.7 reduce_sum.35
  568.8 4.7 fusion.6
  (26 shorter events, 0.3 us)
Async XLA Ops:
  6.5 78.3 %all-gather.6.cloned.1.call-start = ((), (), s32[]{:S(2)}) async-start(), calls=%async_computation.1 | async-start | bytes 17301504 | tf_op jit(solution)/shard_map/all_gather | solution.py:41
  7.3 221.7 %reduce-scatter.2.cloned.1.call-start = ((), (), s32[]{:S(2)}) async-start(), calls=%async_computation.2 | async-start | bytes 10485760 | tf_op jit(solution)/shard_map/reduce_scatter | solution.py:63
  129.6 5.6 copy-start.1
  148.9 80.1 %copy-start.2 = (f32[256]{0:T(256)S(1)}, f32[256]{0:T(256)}, u32[]{:S(2)}) copy-start(f32[256]{0:T(256)} %param.5) | copy-start | bytes 3076
  148.9 106.5 %all-gather.10.cloned.1.call-start = ((), (), s32[]{:S(2)}) async-start(), calls=%async_computation.4 | async-start | bytes 1310720 | tf_op jit(solution)/shard_map/all_gather | solution.py:12
  231.5 299.9 %all-gather.8.cloned.1.call-start = ((), (), s32[]{:S(2)}) async-start(), calls=%async_computation.3 | async-start | bytes 69206016 | tf_op jit(solution)/shard_map/all_gather | solution.py:12
  322.2 2.9 copy-start
Sparse Core Ops, SparseCore 0:
  9.6 75.1 all-gather.5
  149.0 79.8 reduce-scatter.1
  231.6 23.7 all-gather.9
  329.9 201.4 all-gather.7
